TPU v7x, 512 devices: a whole 4x8x8 slice. The times are simulated.
512 devices in a mesh: wide: 64 (over z, x, core), narrow: 8 (over y).
Axes of the slice: x: 4, y: 8, z: 8, core: 2. Of those that a mesh axis runs over, the one named last changes fastest.
Arguments:
- hidden_in: bfloat16 [16384, 2048], P('wide', 'narrow'), may hold values from -6 to 6
- segment_ids: int32 [16384], P('wide'), may hold values from 0 to 31, never falling along the last dimension, each value on 1 to 2048 neighbouring positions
- page_table: int32 [1024], P('wide'), may hold values from 0 to 1023, as said below
- wq: bfloat16 [2048, 2048], P('wide', 'narrow')
- wk: bfloat16 [2048, 2048], P('wide', 'narrow')
- wv: bfloat16 [2048, 2048], P('wide', 'narrow'), may hold values from -0.125 to 0.125
- wo: bfloat16 [2048, 2048], P('narrow', 'wide'), may hold values from -0.125 to 0.125
- wg: bfloat16 [2048, 4096], P('wide', 'narrow'), may hold values from -0.125 to 0.125
- wu: bfloat16 [2048, 4096], P('wide', 'narrow'), may hold values from -0.125 to 0.125
- wd: bfloat16 [4096, 2048], P('narrow', 'wide'), may hold values from -0.09375 to 0.09375
Outputs:
- result: bfloat16 [16384, 2048], P('wide', 'narrow')
- kv_cache: bfloat16 [2, 1024, 16, 2048], P(None, 'wide', None, 'narrow')
Inputs may be any that keep to these rules, and one draw needn't show every extreme that they name: `page_table`: entries 16 * w to 16 * (w + 1) - 1 of the table are a permutation of those same numbers, for every w.
All inputs are finite; a program needn't handle non-finite values.
Results may differ from a plain program's by a relative error of at most 0.017.
Values may be sent and summed in bfloat16 or wider, within the bound.
No kernel may reach another device: no remote copies, remote signals or barrier semaphores. Data moves between devices by JAX's collectives and lax.ppermute only.
A program may use at most 64 MiB of HBM per device.

v0:
```python
import jax
import jax.numpy as jnp
from jax import lax
from jax.sharding import PartitionSpec as P

HEAD_DIM = 128
REACH = 8
PAGE = 16
epsilon = 1e-05
rope_base = 10000.0


def prefix(value, axis, join, neutral):
    count, mine = (lax.axis_size(axis), lax.axis_index(axis))
    pieces = jax.tree.map(lambda part: lax.all_gather(part, axis), value)
    running = jax.tree.map(
        lambda part, zero: jnp.full_like(part, 0) + jnp.asarray(zero, part.dtype), value, neutral
    )

    def lap(position, running):
        longer = join(running, jax.tree.map(lambda part: part[position], pieces))
        return jax.tree.map(lambda new, old: jnp.where(position < mine, new, old), longer, running)

    return lax.fori_loop(0, count - 1, lap, running)


def shifted(value, axis, steps):
    count = lax.axis_size(axis)
    first, last = (max(0, -steps), min(count, count - steps))
    return lax.ppermute(value, axis, [(source, source + steps) for source in range(first, last)])


def norm_rows(source):
    widened = source.astype(jnp.float32)
    center = widened - jnp.mean(widened, axis=-1, keepdims=True)
    spread = jnp.mean(center * center, axis=-1, keepdims=True)
    return (center * lax.rsqrt(spread + epsilon)).astype(jnp.bfloat16)


def rotate(projected, positions):
    head_size = projected.shape[-1]
    half_dim = head_size // 2
    frequency = jnp.power(rope_base, -jnp.arange(half_dim, dtype=jnp.float32) * 2.0 / head_size)
    angles = positions.astype(jnp.float32)[:, None] * frequency[None, :]
    cosine = jnp.cos(angles)[:, None, :]
    sine_part = jnp.sin(angles)[:, None, :]
    first_half = projected[..., :half_dim]
    second_half = projected[..., half_dim:]
    return jnp.concatenate(
        [
            first_half * cosine - second_half * sine_part,
            second_half * cosine + first_half * sine_part,
        ],
        axis=-1,
    )


def join_runs(earlier, later):
    early_last, early_trailing, early_single = earlier
    late_last, late_trailing, late_single = later
    late_empty = late_trailing == 0
    same_id = (early_last == late_last).astype(jnp.int32)
    linked = (late_single == 1) & (same_id == 1) & (early_trailing > 0)
    last_id = jnp.where(late_empty, early_last, late_last)
    trailing = jnp.where(
        late_empty, early_trailing, late_trailing + jnp.where(linked, early_trailing, 0)
    )
    single = jnp.where(
        late_empty,
        early_single,
        jnp.where(early_trailing == 0, late_single, late_single * early_single * same_id),
    )
    return (last_id, trailing, single)


def add_rows(source, piece):
    return jnp.dot(source, piece, preferred_element_type=jnp.float32)


def per_device(hidden_in, segment_ids, page_table, wq, wk, wv, wo, wg, wu, wd):
    tok_rows = hidden_in.shape[0]
    wide_rank = lax.axis_index("wide")
    local_index = jnp.arange(tok_rows, dtype=jnp.int32)
    run_last = segment_ids[tok_rows - 1]
    run_trailing = jnp.sum((segment_ids == run_last).astype(jnp.int32))
    run_single = (segment_ids[0] == run_last).astype(jnp.int32)
    earlier = prefix(
        (run_last, run_trailing, run_single),
        "wide",
        join_runs,
        (jnp.int32(-1), jnp.int32(0), jnp.int32(1)),
    )
    lower_count = jnp.sum((segment_ids[None, :] < segment_ids[:, None]).astype(jnp.int32), axis=1)
    carried = jnp.where(
        (segment_ids == earlier[0]) & (segment_ids == segment_ids[0]), earlier[1], 0
    )
    positions = local_index - lower_count + carried
    global_index = wide_rank * tok_rows + local_index
    query_start = global_index - positions
    whole = lax.all_gather(hidden_in, "narrow", axis=1, tiled=True)
    normed = norm_rows(whole)
    local_width = wq.shape[1]
    head_count = local_width // HEAD_DIM

    def add_normed(piece):
        return add_rows(normed, piece)

    q_proj = add_normed(lax.all_gather(wq, "wide", axis=0, tiled=True))
    k_proj = add_normed(lax.all_gather(wk, "wide", axis=0, tiled=True))
    v_proj = add_normed(lax.all_gather(wv, "wide", axis=0, tiled=True))
    queries = rotate(q_proj.reshape(tok_rows, head_count, HEAD_DIM), positions).astype(jnp.bfloat16)
    keys_rot = rotate(k_proj.reshape(tok_rows, head_count, HEAD_DIM), positions).astype(
        jnp.bfloat16
    )
    values = v_proj.astype(jnp.bfloat16).reshape(tok_rows, head_count, HEAD_DIM)
    current = (keys_rot, values)
    blocks = [current]
    for step_back in range(REACH):
        current = shifted((current[0], current[1]), "wide", 1)
        blocks.append(current)
    score_scale = HEAD_DIM ** (-0.5)
    ordered = blocks[::-1]
    key_all = jnp.concatenate([member[0] for member in ordered], axis=0)
    value_all = jnp.concatenate([member[1] for member in ordered], axis=0)
    key_index = (wide_rank - REACH) * tok_rows + jnp.arange((REACH + 1) * tok_rows, dtype=jnp.int32)
    allowed = (key_index[None, :] >= query_start[:, None]) & (
        key_index[None, :] <= global_index[:, None]
    )
    scores = (
        jnp.einsum("qhd,khd->hqk", queries, key_all, preferred_element_type=jnp.float32)
        * score_scale
    )
    scores = jnp.where(allowed[None], scores, -1e30)
    row_peak = jnp.max(scores, axis=-1, keepdims=True)
    exps = jnp.where(allowed[None], jnp.exp(scores - row_peak), 0.0)
    attn_probs = (exps / jnp.sum(exps, axis=-1, keepdims=True)).astype(jnp.bfloat16)
    mixed = jnp.einsum("hqk,khd->qhd", attn_probs, value_all, preferred_element_type=jnp.float32)
    attended = mixed.astype(jnp.bfloat16).reshape(tok_rows, local_width)
    attn_terms = jnp.dot(
        attended, lax.all_gather(wo, "wide", axis=1, tiled=True), preferred_element_type=jnp.float32
    )
    attn_sum = lax.psum_scatter(
        attn_terms.astype(jnp.bfloat16), "narrow", scatter_dimension=1, tiled=True
    ).astype(jnp.float32)
    first_res = (hidden_in.astype(jnp.float32) + attn_sum).astype(jnp.bfloat16)
    whole_two = lax.all_gather(first_res, "narrow", axis=1, tiled=True)
    normed_two = norm_rows(whole_two)

    def add_second(piece):
        return add_rows(normed_two, piece)

    gate_proj = add_second(lax.all_gather(wg, "wide", axis=0, tiled=True))
    up_proj = add_second(lax.all_gather(wu, "wide", axis=0, tiled=True))
    hidden = (jax.nn.silu(gate_proj) * up_proj).astype(jnp.bfloat16)
    down_terms = jnp.dot(
        hidden, lax.all_gather(wd, "wide", axis=1, tiled=True), preferred_element_type=jnp.float32
    )
    down_sum = lax.psum_scatter(
        down_terms.astype(jnp.bfloat16), "narrow", scatter_dimension=1, tiled=True
    ).astype(jnp.float32)
    result = (first_res.astype(jnp.float32) + down_sum).astype(jnp.bfloat16)
    page_count = tok_rows // PAGE
    slots = page_table - wide_rank * page_count
    pairs = jnp.stack(
        [
            keys_rot.reshape(page_count, PAGE, local_width),
            values.reshape(page_count, PAGE, local_width),
        ],
        axis=0,
    )
    kv_cache = jnp.zeros_like(pairs).at[:, slots].set(pairs)
    return (result, kv_cache)


def solution(mesh):
    return jax.shard_map(
        per_device,
        mesh=mesh,
        in_specs=(
            P("wide", "narrow"),
            P("wide"),
            P("wide"),
            P("wide", "narrow"),
            P("wide", "narrow"),
            P("wide", "narrow"),
            P("narrow", "wide"),
            P("wide", "narrow"),
            P("wide", "narrow"),
            P("narrow", "wide"),
        ),
        out_specs=(P("wide", "narrow"), P(None, "wide", None, "narrow")),
        check_vma=False,
    )
```

profile of v0, /device:TPU:2, one launch (start us, length us, event | category | flops | bytes accessed | tf_op | source)
XLA Modules:
  0.0 878.4 jit_solution(14633172779645840433)
XLA Ops:
  7.2 0.7 all-gather.10.cloned.1.call-update
  7.9 0.7 all-gather.16.cloned.1.call-update
  8.7 0.7 all-gather.12.cloned.1.call-update
  10.0 0.9 convert_reduce_fusion.2
  11.0 1.3 dynamic-slice
  12.3 2.0 fusion.47
  14.3 2.0 fusion.27
  17.6 0.7 dynamic-update-slice.2
  18.3 1.4 dynamic-update-slice
  19.8 25.7 %all-reduce.3 = (s32[64]{0:T(128)S(1)}, s32[64]{0:T(128)S(1)}, s32[64]{0:T(128)S(1)}) all-reduce(s32[64]{0:T(128)S(1)} %dynamic-update-slice, s32[64]{0:T(128)S(1)} %get-tuple-element.159, s32[64]{0:T(128)S(1)} %dynamic-update-slice.2), channel_id=1, replica_groups=mesh['wide'=64,'narrow'=8] {'wide'}, use_global_device_ids=true, to_apply=%add | all-reduce | flops 192 | bytes 1536
  45.5 335.9 %while.15 = (s32[]{:T(128)}, s32[]{:T(128)}, s32[]{:T(128)}, s32[]{:T(128)}, s32[64]{0:T(128)S(1)}, /*index=5*/s32[64]{0:T(128)S(1)}, s32[64]{0:T(128)S(1)}, s32[]{:T(128)}, s32[]{:T(128)}, s32[1]{0:T(128)}) while((s32[]{:T(128)}, s32[]{:T(128)}, s32[]{:T(128)}, s32[]{:T(128)}, s32[64]{0:T(128)S(1)}, /*index=5*/s32[64]{0:T(128)S(1)}, ...), condition=%wide.region_5.6_spmd, body=%wide.region_4.5_spmd.sunk | while | flops 17 | bytes 279 | solution.py:24
  52.1 0.7 dynamic_slice.26
  57.4 0.7 dynamic_slice.26
  62.7 0.7 dynamic_slice.26
  68.1 0.7 dynamic_slice.26
  73.4 0.7 dynamic_slice.26
  381.3 1.3 fusion.43
  383.2 1.5 convert_reduce_fusion.1
  385.6 1.7 fusion.52
  387.8 1.9 collective-permute-start.8
  389.8 1.7 convolution_convert_fusion.2
  391.6 2.5 collective-permute-start
  394.1 1.9 collective-permute-start.9
  396.1 1.8 collective-permute-done
  397.9 1.9 collective-permute-start.1
  400.4 1.9 collective-permute-start.10
  402.4 1.7 collective-permute-done.1
  404.1 1.9 collective-permute-start.2
  406.7 1.9 collective-permute-start.11
  408.6 1.8 collective-permute-done.2
  410.4 2.2 collective-permute-start.3
  413.1 3.3 collective-permute-start.12
  416.9 4.6 collective-permute-start.4
  421.6 3.6 collective-permute-start.13
  425.2 1.7 fusion.51
  427.0 4.6 collective-permute-start.5
  431.7 3.7 collective-permute-start.14
  435.7 4.7 collective-permute-start.6
  440.4 3.2 collective-permute-start.15
  443.6 0.8 subtract_convert_fusion
  444.4 5.0 collective-permute-start.7
  449.4 0.9 constant_dynamic-update-slice_fusion.15
  450.3 0.9 constant_dynamic-update-slice_fusion.14
  451.3 0.9 constant_dynamic-update-slice_fusion.13
  452.5 1.4 constant_dynamic-update-slice_fusion.5
  454.0 1.0 copy-done.8
  455.0 5.9 fusion.48
  460.9 3.7 fusion.15
  464.6 22.8 %all-gather.18.cloned.1.call-done = bf16[256,2048]{0,1:T(8,128)(2,1)} async-done(((bf16[256,32]{0,1:T(8,128)(2,1)}), bf16[256,2048]{0,1:T(8,128)(2,1)}) %all-gather.18.cloned.1.call-update) | async-done | bytes 1048592 | tf_op jit(solution)/shard_map/all_gather | solution.py:140
  487.4 2.7 convolution_convert_fusion.1
  490.2 39.1 %reduce-scatter.3.cloned.1.call-done = bf16[256,256]{1,0:T(8,128)(2,1)} async-done(((bf16[256,2048]{1,0:T(8,128)(2,1)}), bf16[256,256]{1,0:T(8,128)(2,1)}) %reduce-scatter.3.cloned.1.call-update) | async-done | bytes 131088 | tf_op jit(solution)/shard_map/reduce_scatter | solution.py:142
  529.3 1.6 add_convert_fusion.1
  531.0 0.7 all-gather.22.cloned.1.call-update
  531.7 0.7 all-gather.24.cloned.1.call-update
  533.2 40.0 %all-gather.20.cloned.1.call-done = bf16[256,2048]{1,0:T(8,128)(2,1)} async-done(((bf16[256,256]{1,0:T(8,128)(2,1)}), bf16[256,2048]{1,0:T(8,128)(2,1)}) %all-gather.20.cloned.1.call-update) | async-done | bytes 1048592 | tf_op jit(solution)/shard_map/all_gather | solution.py:146
  573.2 1.5 convert_reduce_fusion
  575.2 83.4 %all-gather.22.cloned.1.call-done = bf16[2048,512]{1,0:T(8,128)(2,1)} async-done(((bf16[32,512]{1,0:T(8,128)(2,1)}), bf16[2048,512]{1,0:T(8,128)(2,1)}) %all-gather.22.cloned.1.call-update) | async-done | bytes 2097168 | tf_op jit(solution)/shard_map/all_gather | solution.py:152
  658.6 2.3 fusion.41
  660.9 81.6 %all-gather.24.cloned.1.call-done = bf16[2048,512]{1,0:T(8,128)(2,1)} async-done(((bf16[32,512]{1,0:T(8,128)(2,1)}), bf16[2048,512]{1,0:T(8,128)(2,1)}) %all-gather.24.cloned.1.call-update) | async-done | bytes 2097168 | tf_op jit(solution)/shard_map/all_gather | solution.py:153
  742.6 83.8 %all-gather.26.cloned.1.call-done = bf16[512,2048]{0,1:T(8,128)(2,1)} async-done(((bf16[512,32]{0,1:T(8,128)(2,1)}), bf16[512,2048]{0,1:T(8,128)(2,1)}) %all-gather.26.cloned.1.call-update) | async-done | bytes 2097168 | tf_op jit(solution)/shard_map/all_gather | solution.py:156
  826.4 4.7 convolution_convert_fusion
  831.5 1.2 scatter_fusion
  832.7 37.6 %reduce-scatter.5.cloned.1.call-done = bf16[256,256]{1,0:T(8,128)(2,1)} async-done(((bf16[256,2048]{1,0:T(8,128)(2,1)}), bf16[256,256]{1,0:T(8,128)(2,1)}) %reduce-scatter.5.cloned.1.call-update) | async-done | bytes 131088 | tf_op jit(solution)/shard_map/reduce_scatter | solution.py:158
  870.3 1.6 add_convert_fusion
  (281 shorter events, 127.9 us)
Async XLA Ops:
  7.2 376.1 %all-gather.10.cloned.1.call-start = ((), (), s32[]{:S(2)}) async-start(), calls=%async_computation.2 | async-start | bytes 1179648 | tf_op jit(solution)/shard_map/all_gather | solution.py:100
  7.9 377.7 %all-gather.16.cloned.1.call-start = ((), (), s32[]{:S(2)}) async-start(), calls=%async_computation.5 | async-start | bytes 1064960 | tf_op jit(solution)/shard_map/all_gather | solution.py:109
  8.6 381.1 %all-gather.12.cloned.1.call-start = ((), (), s32[]{:S(2)}) async-start(), calls=%async_computation.3 | async-start | bytes 1064960 | tf_op jit(solution)/shard_map/all_gather | solution.py:110
  9.4 415.9 %all-gather.14.cloned.1.call-start = ((), (), s32[]{:S(2)}) async-start(), calls=%async_computation.4 | async-start | bytes 1064960 | tf_op jit(solution)/shard_map/all_gather | solution.py:108
  10.0 477.4 %all-gather.18.cloned.1.call-start = ((), (), s32[]{:S(2)}) async-start(), calls=%async_computation.6 | async-start | bytes 1064960 | tf_op jit(solution)/shard_map/all_gather | solution.py:140
  383.2 1.6 copy-start
  387.8 6.3 collective-permute-start.8
  391.6 6.3 collective-permute-start
  394.1 6.3 collective-permute-start.9
  397.9 6.3 collective-permute-start.1
  400.4 6.3 collective-permute-start.10
  402.4 126.9 %reduce-scatter.3.cloned.1.call-start = ((), (), s32[]{:S(2)}) async-start(), calls=%async_computation.7 | async-start | bytes 1179648 | tf_op jit(solution)/shard_map/reduce_scatter | solution.py:142
  404.1 6.3 collective-permute-start.2
  406.7 6.4 collective-permute-start.11
  410.4 6.5 collective-permute-start.3
  413.1 8.5 collective-permute-start.12
  416.9 10.1 %collective-permute-start.4 = (bf16[256,2,128]{0,2,1:T(8,128)(2,1)S(1)}, bf16[256,2,128]{0,2,1:T(8,128)(2,1)}, u32[]{:S(2)}, u32[]{:S(2)}) collective-permute-start(bf16[256,2,128]{0,2,1:T(8,128)(2,1)S(1)} %collective-permute-done.3), channel_id=1, source_target_pairs={{0,8},{8,16},{16,24},{24,32},{32,40},{40,48},{48,56},{56,64},{64,7... | collective-permute-start | bytes 393224 | tf_op jit(solution)/shard_map/ppermute | solution.py:30
  421.6 10.1 %collective-permute-start.13 = (bf16[256,2,128]{2,0,1:T(8,128)(2,1)}, bf16[256,2,128]{2,0,1:T(8,128)(2,1)}, u32[]{:S(2)}, u32[]{:S(2)}) collective-permute-start(bf16[256,2,128]{2,0,1:T(8,128)(2,1)} %collective-permute-done.12), channel_id=1, source_target_pairs={{0,8},{8,16},{16,24},{24,32},{32,40},{40,48},{48,56},{56,64},{64,7... | collective-permute-start | bytes 393224 | tf_op jit(solution)/shard_map/ppermute | solution.py:30
  427.0 8.6 collective-permute-start.5
  431.7 8.7 collective-permute-start.14
  435.7 8.7 collective-permute-start.6
  440.4 8.9 %collective-permute-start.15 = (bf16[256,2,128]{2,0,1:T(8,128)(2,1)S(1)}, bf16[256,2,128]{2,0,1:T(8,128)(2,1)S(1)}, u32[]{:S(2)}, u32[]{:S(2)}) collective-permute-start(bf16[256,2,128]{2,0,1:T(8,128)(2,1)S(1)} %collective-permute-done.14), channel_id=1, source_target_pairs={{0,8},{8,16},{16,24},{24,32},{32,40},{40,48},{48,56},{56,64},{64,7... | collective-permute-start | bytes 393224 | tf_op jit(solution)/shard_map/ppermute | solution.py:30
  444.4 8.1 collective-permute-start.7
  452.4 1.6 copy-start.7
  452.4 2.6 copy-start.5
  452.4 2.6 copy-start.6
  454.0 1.0 copy-start.8
  487.4 41.9 %copy-start.4 = (bf16[256,256]{1,0:T(8,128)(2,1)S(1)}, bf16[256,256]{1,0:T(8,128)(2,1)}, u32[]{:S(2)}) copy-start(bf16[256,256]{1,0:T(8,128)(2,1)} %param.12) | copy-start | bytes 393220
  490.1 83.1 %all-gather.20.cloned.1.call-start = ((), (), s32[]{:S(2)}) async-start(), calls=%async_computation.8 | async-start | bytes 1179648 | tf_op jit(solution)/shard_map/all_gather | solution.py:146
  530.9 127.7 %all-gather.22.cloned.1.call-start = ((), (), s32[]{:S(2)}) async-start(), calls=%async_computation.9 | async-start | bytes 2129920 | tf_op jit(solution)/shard_map/all_gather | solution.py:152
  531.7 210.9 %all-gather.24.cloned.1.call-start = ((), (), s32[]{:S(2)}) async-start(), calls=%async_computation.10 | async-start | bytes 2129920 | tf_op jit(solution)/shard_map/all_gather | solution.py:153
  532.4 294.0 %all-gather.26.cloned.1.call-start = ((), (), s32[]{:S(2)}) async-start(), calls=%async_computation.11 | async-start | bytes 2129920 | tf_op jit(solution)/shard_map/all_gather | solution.py:156
  533.0 337.3 %reduce-scatter.5.cloned.1.call-start = ((), (), s32[]{:S(2)}) async-start(), calls=%async_computation.12 | async-start | bytes 1179648 | tf_op jit(solution)/shard_map/reduce_scatter | solution.py:158
  573.2 1.5 copy-start.1
  660.9 170.2 %copy-start.9 = (s32[16]{0:T(128)S(1)}, s32[16]{0:T(128)}, u32[]{:S(2)}) copy-start(s32[16]{0:T(128)} %param.14) | copy-start | bytes 196
  831.3 39.0 %copy-start.2 = (bf16[256,256]{1,0:T(8,128)(2,1)S(1)}, bf16[256,256]{1,0:T(8,128)(2,1)}, u32[]{:S(2)}) copy-start(bf16[256,256]{1,0:T(8,128)(2,1)} %add_convert_fusion.1) | copy-start | bytes 393220
  832.7 39.2 %copy-start.3 = (bf16[2,16,16,256]{3,2,1,0:T(8,128)(2,1)}, bf16[2,16,16,256]{3,2,1,0:T(8,128)(2,1)S(1)}, u32[]{:S(2)}) copy-start(bf16[2,16,16,256]{3,2,1,0:T(8,128)(2,1)S(1)} %scatter_fusion) | copy-start | bytes 786436
Sparse Core Ops, SparseCore 0:
  10.0 46.6 all-gather.9
  60.1 81.1 all-gather.15
  144.6 79.8 all-gather.11
  227.7 79.7 all-gather.13
  402.5 84.8 all-gather.17
  490.2 38.9 reduce-scatter.2
  531.9 41.2 all-gather.19
  576.6 81.9 all-gather.21
  661.9 80.5 all-gather.23
  745.8 80.5 all-gather.25
  831.2 39.0 reduce-scatter.4
where the time goes:
time: 882 us; the launch traced here: 878 us
  waiting for transfers between devices  400 us (45%)
  loops' own time  212 us (24%)
  local copies, waits for them, and re-layouts  137 us (16%)
  starting transfers between devices  49.6 us (6%)
  blocking collectives  25.7 us (3%)
  matrix products  24.5 us (3%)
  between operations  15.8 us (2%)
  other arithmetic  13.9 us (2%)
    another operation x1, loops' own time, prefix(): return lax.fori_loop(0, count - 1, lap, running)  212 us
    dynamic_slice x189, local copies, waits for them, and re-layouts, lap(): longer = join(running, jax.tree.map(lambda part: part[position], pieces))  124 us
    all_gather x1, waiting for transfers between devices, per_device(): lax.all_gather(wd, 'wide', axis=1, tiled=True)  83.8 us
    all_gather x1, waiting for transfers between devices, per_device(): gate_proj = add_second(lax.all_gather(wg, 'wide', axis=0, tiled=True))  83.4 us
    all_gather x1, waiting for transfers between devices, per_device(): up_proj = add_second(lax.all_gather(wu, 'wide', axis=0, tiled=True))  81.6 us
    ppermute x16, starting transfers between devices, shifted(): lax.ppermute(value, axis, [(source, source + steps) for source in range(f...  49 us
    all_gather x1, waiting for transfers between devices, per_device(): whole_two = lax.all_gather(first_res, 'narrow', axis=1, tiled=True)  40 us
    reduce_scatter x1, waiting for transfers between devices, per_device(): lax.psum_scatter(attn_terms.astype(jnp.bfloat16), 'narrow', scatter_dimen...  39.1 us
  transfers between devices with their start and end apart: 27, of which 13 were waited for; matrix products, arithmetic and copies ran while one was open for 19% of the time, Pallas kernels for 0%

commit v1 on v0

--- a/solution.py
+++ b/solution.py
@@ -8,6 +8,12 @@
 PAGE = 16
 epsilon = 1e-05
 rope_base = 10000.0
+
+
+def laid_out(blocks, dim):
+    dims = list(blocks.shape[1:])
+    dims[dim] *= blocks.shape[0]
+    return jnp.moveaxis(blocks, 0, dim).reshape(dims)
 
 
 def prefix(value, axis, join, neutral):
@@ -143,7 +149,19 @@
         attn_terms.astype(jnp.bfloat16), "narrow", scatter_dimension=1, tiled=True
     ).astype(jnp.float32)
     first_res = (hidden_in.astype(jnp.float32) + attn_sum).astype(jnp.bfloat16)
-    whole_two = lax.all_gather(first_res, "narrow", axis=1, tiled=True)
+    length = lax.axis_size("narrow")
+    pairs_2 = [(i, (i + 1) % length) for i in range(length)]
+    back = [(b, a) for a, b in pairs_2]
+    lower, upper = ([], [])
+    for turn in range(length - 1):
+        if turn % 2 == 0:
+            lower.append(lax.ppermute(lower[-1] if lower else first_res, "narrow", pairs_2))
+        else:
+            upper.append(lax.ppermute(upper[-1] if upper else first_res, "narrow", back))
+    pieces_2 = jnp.stack([*lower[::-1], first_res, *upper])
+    shift = lax.axis_index("narrow") - len(lower)
+    pieces_2 = pieces_2[(jnp.arange(length) - shift) % length]
+    whole_two = laid_out(pieces_2, 1)
     normed_two = norm_rows(whole_two)
 
     def add_second(piece):

time: 882 us -> 820 us (0.930)
  the two profiles are of different devices: /device:TPU:2 before, /device:TPU:4 now
where the time goes in v1:
time: 820 us; the launch traced here: 815 us
  waiting for transfers between devices  323 us (39%)
  loops' own time  200 us (24%)
  local copies, waits for them, and re-layouts  132 us (16%)
  starting transfers between devices  81.7 us (10%)
  blocking collectives  24.7 us (3%)
  matrix products  24.1 us (3%)
  between operations  16.3 us (2%)
  other arithmetic  13.8 us (2%)
    another operation x1, loops' own time, prefix(): return lax.fori_loop(0, count - 1, lap, running)  200 us
    dynamic_slice x189, local copies, waits for them, and re-layouts, lap(): longer = join(running, jax.tree.map(lambda part: part[position], pieces))  117 us
    all_gather x1, waiting for transfers between devices, per_device(): lax.all_gather(wd, 'wide', axis=1, tiled=True)  84 us
    all_gather x1, waiting for transfers between devices, per_device(): up_proj = add_second(lax.all_gather(wu, 'wide', axis=0, tiled=True))  81.6 us
    ppermute x16, starting transfers between devices, shifted(): lax.ppermute(value, axis, [(source, source + steps) for source in range(f...  56.8 us
    all_gather x1, waiting for transfers between devices, per_device(): gate_proj = add_second(lax.all_gather(wg, 'wide', axis=0, tiled=True))  43.5 us
    reduce_scatter x1, waiting for transfers between devices, per_device(): lax.psum_scatter(attn_terms.astype(jnp.bfloat16), 'narrow', scatter_dimen...  37.8 us
    reduce_scatter x1, waiting for transfers between devices, per_device(): lax.psum_scatter(down_terms.astype(jnp.bfloat16), 'narrow', scatter_dimen...  37.7 us
  transfers between devices with their start and end apart: 33, of which 13 were waited for; matrix products, arithmetic and copies ran while one was open for 20% of the time, Pallas kernels for 0%

profile of v1, /device:TPU:4, one launch (start us, length us, event | category | flops | bytes accessed | tf_op | source)
XLA Modules:
  0.0 815.2 jit_solution(16800686309239877116)
XLA Ops:
  7.9 0.7 all-gather.15.cloned.1.call-update
  10.0 0.9 convert_reduce_fusion.2
  11.0 1.2 dynamic-slice
  12.2 1.9 fusion.45
  14.1 2.0 fusion.27
  18.1 1.3 dynamic-update-slice
  19.4 24.7 %all-reduce.3 = (s32[64]{0:T(128)S(1)}, s32[64]{0:T(128)S(1)}, s32[64]{0:T(128)S(1)}) all-reduce(s32[64]{0:T(128)S(1)} %dynamic-update-slice, s32[64]{0:T(128)S(1)} %get-tuple-element.159, s32[64]{0:T(128)S(1)} %dynamic-update-slice.2), channel_id=1, replica_groups=mesh['wide'=64,'narrow'=8] {'wide'}, use_global_device_ids=true, to_apply=%add | all-reduce | flops 192 | bytes 1536
  44.1 316.6 %while.15 = (s32[]{:T(128)}, s32[]{:T(128)}, s32[]{:T(128)}, s32[]{:T(128)}, s32[64]{0:T(128)S(1)}, /*index=5*/s32[64]{0:T(128)S(1)}, s32[64]{0:T(128)S(1)}, s32[]{:T(128)}, s32[]{:T(128)}, s32[1]{0:T(128)}) while((s32[]{:T(128)}, s32[]{:T(128)}, s32[]{:T(128)}, s32[]{:T(128)}, s32[64]{0:T(128)S(1)}, /*index=5*/s32[64]{0:T(128)S(1)}, ...), condition=%wide.region_5.6_spmd, body=%wide.region_4.5_spmd.sunk | while | flops 17 | bytes 279 | solution.py:30
  360.8 1.3 fusion.41
  362.7 1.5 convert_reduce_fusion.1
  365.0 1.7 fusion.50
  367.3 1.9 collective-permute-start.8
  369.2 1.7 convolution_convert_fusion.2
  371.0 3.5 collective-permute-start
  374.5 1.9 collective-permute-start.9
  376.4 0.9 collective-permute-done
  377.3 3.6 collective-permute-start.1
  380.9 1.9 collective-permute-start.10
  383.6 4.0 collective-permute-start.2
  387.5 3.7 collective-permute-start.11
  391.3 4.6 collective-permute-start.3
  396.0 3.6 collective-permute-start.12
  400.2 4.6 collective-permute-start.4
  404.8 3.7 collective-permute-start.13
  408.5 1.7 fusion.49
  410.3 4.7 collective-permute-start.5
  415.1 3.1 collective-permute-start.14
  418.5 5.0 collective-permute-start.6
  423.6 1.9 collective-permute-start.15
  425.5 0.8 subtract_convert_fusion
  426.3 5.0 collective-permute-start.7
  431.3 0.9 constant_dynamic-update-slice_fusion.15
  432.2 0.9 constant_dynamic-update-slice_fusion.14
  433.2 0.9 constant_dynamic-update-slice_fusion.13
  434.4 1.4 constant_dynamic-update-slice_fusion.5
  435.9 1.0 copy-done.6
  436.9 6.0 fusion.46
  442.9 3.3 fusion.15
  446.2 21.5 %all-gather.17.cloned.1.call-done = bf16[256,2048]{0,1:T(8,128)(2,1)} async-done(((bf16[256,32]{0,1:T(8,128)(2,1)}), bf16[256,2048]{0,1:T(8,128)(2,1)}) %all-gather.17.cloned.1.call-update) | async-done | bytes 1048592 | tf_op jit(solution)/shard_map/all_gather | solution.py:146
  467.7 2.8 convolution_convert_fusion.1
  470.5 0.7 all-gather.19.cloned.1.call-update
  472.0 37.8 %reduce-scatter.3.cloned.1.call-done = bf16[256,256]{1,0:T(8,128)(2,1)} async-done(((bf16[256,2048]{1,0:T(8,128)(2,1)}), bf16[256,256]{1,0:T(8,128)(2,1)}) %reduce-scatter.3.cloned.1.call-update) | async-done | bytes 131088 | tf_op jit(solution)/shard_map/reduce_scatter | solution.py:148
  509.8 0.9 add_convert_fusion.1
  510.8 2.9 collective-permute-start.16
  513.7 5.2 collective-permute-done.16
  518.8 2.4 collective-permute-start.17
  521.3 4.6 collective-permute-start.20
  525.9 2.1 collective-permute-done.17
  528.0 1.9 collective-permute-start.18
  530.1 5.2 collective-permute-start.21
  535.3 1.4 collective-permute-done.18
  536.7 1.9 collective-permute-start.19
  538.6 5.5 collective-permute-start.22
  544.8 1.6 collective-permute-done.22
  547.0 1.6 convert_bitcast_fusion
  548.6 1.9 copy.34
  551.4 43.5 %all-gather.19.cloned.1.call-done = bf16[2048,512]{1,0:T(8,128)(2,1)} async-done(((bf16[32,512]{1,0:T(8,128)(2,1)}), bf16[2048,512]{1,0:T(8,128)(2,1)}) %all-gather.19.cloned.1.call-update) | async-done | bytes 2097168 | tf_op jit(solution)/shard_map/all_gather | solution.py:170
  594.9 2.3 fusion.51
  597.2 81.6 %all-gather.21.cloned.1.call-done = bf16[2048,512]{1,0:T(8,128)(2,1)} async-done(((bf16[32,512]{1,0:T(8,128)(2,1)}), bf16[2048,512]{1,0:T(8,128)(2,1)}) %all-gather.21.cloned.1.call-update) | async-done | bytes 2097168 | tf_op jit(solution)/shard_map/all_gather | solution.py:171
  678.9 84.0 %all-gather.23.cloned.1.call-done = bf16[512,2048]{0,1:T(8,128)(2,1)} async-done(((bf16[512,32]{0,1:T(8,128)(2,1)}), bf16[512,2048]{0,1:T(8,128)(2,1)}) %all-gather.23.cloned.1.call-update) | async-done | bytes 2097168 | tf_op jit(solution)/shard_map/all_gather | solution.py:174
  762.9 4.6 convolution_convert_fusion
  767.8 1.2 scatter_fusion
  769.1 37.7 %reduce-scatter.5.cloned.1.call-done = bf16[256,256]{1,0:T(8,128)(2,1)} async-done(((bf16[256,2048]{1,0:T(8,128)(2,1)}), bf16[256,256]{1,0:T(8,128)(2,1)}) %reduce-scatter.5.cloned.1.call-update) | async-done | bytes 131088 | tf_op jit(solution)/shard_map/reduce_scatter | solution.py:176
  806.7 1.6 add_convert_fusion
  (304 shorter events, 127.2 us)
Async XLA Ops:
  7.2 355.5 %all-gather.9.cloned.1.call-start = ((), (), s32[]{:S(2)}) async-start(), calls=%async_computation.2 | async-start | bytes 1179648 | tf_op jit(solution)/shard_map/all_gather | solution.py:106
  7.9 357.1 %all-gather.15.cloned.1.call-start = ((), (), s32[]{:S(2)}) async-start(), calls=%async_computation.5 | async-start | bytes 1064960 | tf_op jit(solution)/shard_map/all_gather | solution.py:115
  8.6 360.6 %all-gather.11.cloned.1.call-start = ((), (), s32[]{:S(2)}) async-start(), calls=%async_computation.3 | async-start | bytes 1064960 | tf_op jit(solution)/shard_map/all_gather | solution.py:116
  9.4 399.1 %all-gather.13.cloned.1.call-start = ((), (), s32[]{:S(2)}) async-start(), calls=%async_computation.4 | async-start | bytes 1064960 | tf_op jit(solution)/shard_map/all_gather | solution.py:114
  10.0 457.7 %all-gather.17.cloned.1.call-start = ((), (), s32[]{:S(2)}) async-start(), calls=%async_computation.6 | async-start | bytes 1064960 | tf_op jit(solution)/shard_map/all_gather | solution.py:146
  362.7 1.6 copy-start
  367.3 7.2 collective-permute-start.8
  371.0 6.3 collective-permute-start
  374.5 6.4 collective-permute-start.9
  377.3 6.3 collective-permute-start.1
  380.9 6.7 collective-permute-start.10
  382.8 127.0 %reduce-scatter.3.cloned.1.call-start = ((), (), s32[]{:S(2)}) async-start(), calls=%async_computation.7 | async-start | bytes 1179648 | tf_op jit(solution)/shard_map/reduce_scatter | solution.py:148
  383.6 7.7 collective-permute-start.2
  387.5 8.4 %collective-permute-start.11 = (bf16[256,2,128]{2,0,1:T(8,128)(2,1)S(1)}, bf16[256,2,128]{2,0,1:T(8,128)(2,1)}, u32[]{:S(2)}, u32[]{:S(2)}) collective-permute-start(bf16[256,2,128]{2,0,1:T(8,128)(2,1)S(1)} %collective-permute-done.10), channel_id=1, source_target_pairs={{0,8},{8,16},{16,24},{24,32},{32,40},{40,48},{48,56},{56,64},{64,7... | collective-permute-start | bytes 393224 | tf_op jit(solution)/shard_map/ppermute | solution.py:36
  391.3 8.8 %collective-permute-start.3 = (bf16[256,2,128]{0,2,1:T(8,128)(2,1)S(1)}, bf16[256,2,128]{0,2,1:T(8,128)(2,1)S(1)}, u32[]{:S(2)}, u32[]{:S(2)}) collective-permute-start(bf16[256,2,128]{0,2,1:T(8,128)(2,1)S(1)} %collective-permute-done.2), channel_id=1, source_target_pairs={{0,8},{8,16},{16,24},{24,32},{32,40},{40,48},{48,56},{56,64},{64,7... | collective-permute-start | bytes 393224 | tf_op jit(solution)/shard_map/ppermute | solution.py:36
  396.0 8.9 %collective-permute-start.12 = (bf16[256,2,128]{2,0,1:T(8,128)(2,1)}, bf16[256,2,128]{2,0,1:T(8,128)(2,1)}, u32[]{:S(2)}, u32[]{:S(2)}) collective-permute-start(bf16[256,2,128]{2,0,1:T(8,128)(2,1)} %collective-permute-done.11), channel_id=1, source_target_pairs={{0,8},{8,16},{16,24},{24,32},{32,40},{40,48},{48,56},{56,64},{64,7... | collective-permute-start | bytes 393224 | tf_op jit(solution)/shard_map/ppermute | solution.py:36
  400.2 10.1 %collective-permute-start.4 = (bf16[256,2,128]{0,2,1:T(8,128)(2,1)S(1)}, bf16[256,2,128]{0,2,1:T(8,128)(2,1)}, u32[]{:S(2)}, u32[]{:S(2)}) collective-permute-start(bf16[256,2,128]{0,2,1:T(8,128)(2,1)S(1)} %collective-permute-done.3), channel_id=1, source_target_pairs={{0,8},{8,16},{16,24},{24,32},{32,40},{40,48},{48,56},{56,64},{64,7... | collective-permute-start | bytes 393224 | tf_op jit(solution)/shard_map/ppermute | solution.py:36
  404.8 10.2 %collective-permute-start.13 = (bf16[256,2,128]{2,0,1:T(8,128)(2,1)}, bf16[256,2,128]{2,0,1:T(8,128)(2,1)}, u32[]{:S(2)}, u32[]{:S(2)}) collective-permute-start(bf16[256,2,128]{2,0,1:T(8,128)(2,1)} %collective-permute-done.12), channel_id=1, source_target_pairs={{0,8},{8,16},{16,24},{24,32},{32,40},{40,48},{48,56},{56,64},{64,7... | collective-permute-start | bytes 393224 | tf_op jit(solution)/shard_map/ppermute | solution.py:36
  410.3 8.2 %collective-permute-start.5 = (bf16[256,2,128]{0,2,1:T(8,128)(2,1)}, bf16[256,2,128]{0,2,1:T(8,128)(2,1)S(1)}, u32[]{:S(2)}, u32[]{:S(2)}) collective-permute-start(bf16[256,2,128]{0,2,1:T(8,128)(2,1)} %collective-permute-done.4), channel_id=1, source_target_pairs={{0,8},{8,16},{16,24},{24,32},{32,40},{40,48},{48,56},{56,64},{64,7... | collective-permute-start | bytes 393224 | tf_op jit(solution)/shard_map/ppermute | solution.py:36
  415.1 8.5 %collective-permute-start.14 = (bf16[256,2,128]{2,0,1:T(8,128)(2,1)}, bf16[256,2,128]{2,0,1:T(8,128)(2,1)S(1)}, u32[]{:S(2)}, u32[]{:S(2)}) collective-permute-start(bf16[256,2,128]{2,0,1:T(8,128)(2,1)} %collective-permute-done.13), channel_id=1, source_target_pairs={{0,8},{8,16},{16,24},{24,32},{32,40},{40,48},{48,56},{56,64},{64,7... | collective-permute-start | bytes 393224 | tf_op jit(solution)/shard_map/ppermute | solution.py:36
  418.5 7.7 collective-permute-start.6
  423.6 7.7 collective-permute-start.15
  426.3 8.1 collective-permute-start.7
  434.3 1.6 copy-start.5
  434.3 2.6 copy-start.3
  434.3 2.6 copy-start.4
  435.9 1.0 copy-start.6
  436.9 6.0 copy-start.7
  467.7 42.1 %copy-start.2 = (bf16[256,256]{1,0:T(8,128)(2,1)S(1)}, bf16[256,256]{1,0:T(8,128)(2,1)}, u32[]{:S(2)}) copy-start(bf16[256,256]{1,0:T(8,128)(2,1)} %param.12) | copy-start | bytes 393220
  470.5 124.4 %all-gather.19.cloned.1.call-start = ((), (), s32[]{:S(2)}) async-start(), calls=%async_computation.8 | async-start | bytes 2129920 | tf_op jit(solution)/shard_map/all_gather | solution.py:170
  471.2 207.6 %all-gather.21.cloned.1.call-start = ((), (), s32[]{:S(2)}) async-start(), calls=%async_computation.9 | async-start | bytes 2129920 | tf_op jit(solution)/shard_map/all_gather | solution.py:171
  472.0 290.9 %all-gather.23.cloned.1.call-start = ((), (), s32[]{:S(2)}) async-start(), calls=%async_computation.10 | async-start | bytes 2129920 | tf_op jit(solution)/shard_map/all_gather | solution.py:174
  510.8 8.1 collective-permute-start.16
  518.8 9.2 %collective-permute-start.17 = (bf16[256,256]{1,0:T(8,128)(2,1)S(1)}, bf16[256,256]{1,0:T(8,128)(2,1)S(1)}, u32[]{:S(2)}, u32[]{:S(2)}) collective-permute-start(bf16[256,256]{1,0:T(8,128)(2,1)S(1)} %collective-permute-done.16), channel_id=1, source_target_pairs={{0,1},{1,2},{2,3},{3,4},{4,5},{5,6},{6,7},{7,0},{8,9},{9,10},{10,1... | collective-permute-start | bytes 393224 | tf_op jit(solution)/shard_map/ppermute | solution.py:158
  521.3 8.8 %collective-permute-start.20 = (bf16[256,256]{1,0:T(8,128)(2,1)S(1)}, bf16[256,256]{1,0:T(8,128)(2,1)S(1)}, u32[]{:S(2)}, u32[]{:S(2)}) collective-permute-start(bf16[256,256]{1,0:T(8,128)(2,1)S(1)} %add_convert_fusion.1), channel_id=1, source_target_pairs={{1,0},{2,1},{3,2},{4,3},{5,4},{6,5},{7,6},{0,7},{9,8},{10,9},{11,1... | collective-permute-start | bytes 393224 | tf_op jit(solution)/shard_map/ppermute | solution.py:160
  528.0 8.6 %collective-permute-start.18 = (bf16[256,256]{1,0:T(8,128)(2,1)S(1)}, bf16[256,256]{1,0:T(8,128)(2,1)S(1)}, u32[]{:S(2)}, u32[]{:S(2)}) collective-permute-start(bf16[256,256]{1,0:T(8,128)(2,1)S(1)} %collective-permute-done.17), channel_id=1, source_target_pairs={{0,1},{1,2},{2,3},{3,4},{4,5},{5,6},{6,7},{7,0},{8,9},{9,10},{10,1... | collective-permute-start | bytes 393224 | tf_op jit(solution)/shard_map/ppermute | solution.py:158
  530.0 276.7 %reduce-scatter.5.cloned.1.call-start = ((), (), s32[]{:S(2)}) async-start(), calls=%async_computation.11 | async-start | bytes 1179648 | tf_op jit(solution)/shard_map/reduce_scatter | solution.py:176
  530.1 8.6 %collective-permute-start.21 = (bf16[256,256]{1,0:T(8,128)(2,1)S(1)}, bf16[256,256]{1,0:T(8,128)(2,1)S(1)}, u32[]{:S(2)}, u32[]{:S(2)}) collective-permute-start(bf16[256,256]{1,0:T(8,128)(2,1)S(1)} %collective-permute-done.20), channel_id=1, source_target_pairs={{1,0},{2,1},{3,2},{4,3},{5,4},{6,5},{7,6},{0,7},{9,8},{10,9},{11,1... | collective-permute-start | bytes 393224 | tf_op jit(solution)/shard_map/ppermute | solution.py:160
  536.7 8.1 collective-permute-start.19
  538.6 7.8 collective-permute-start.22
  597.2 170.3 %copy-start.8 = (s32[16]{0:T(128)S(1)}, s32[16]{0:T(128)}, u32[]{:S(2)}) copy-start(s32[16]{0:T(128)} %param.14) | copy-start | bytes 196
  769.1 39.3 %copy-start.1 = (bf16[2,16,16,256]{3,2,1,0:T(8,128)(2,1)}, bf16[2,16,16,256]{3,2,1,0:T(8,128)(2,1)S(1)}, u32[]{:S(2)}) copy-start(bf16[2,16,16,256]{3,2,1,0:T(8,128)(2,1)S(1)} %scatter_fusion) | copy-start | bytes 786436
Sparse Core Ops, SparseCore 0:
  10.0 46.5 all-gather.8
  60.0 81.2 all-gather.14
  144.6 79.7 all-gather.10
  227.6 79.7 all-gather.12
  382.9 84.7 all-gather.16
  470.6 39.1 reduce-scatter.2
  513.2 81.6 all-gather.18
  598.3 80.5 all-gather.20
  682.2 80.5 all-gather.22
  767.6 39.0 reduce-scatter.4
